TPU v7x, 32 devices: a whole 2x2x4 slice. The times are simulated.
32 devices in a mesh: row: 16 (over z, y, x), col: 2 (over core).
Axes of the slice: x: 2, y: 2, z: 4, core: 2. Of those that a mesh axis runs over, the one named last changes fastest.
Arguments:
- matrix: bfloat16 [16384, 2048], P('row', 'col'), may hold values from -6 to 6
- fill_mask: int32 [64, 16], P('row', 'col'), may hold values from 0 to 1, as said below
- col_rows: int32 [16], replicated, may hold values from 0 to 127, as said below
- inverses: bfloat16 [2, 128, 128], replicated, may hold values from -0.05 to 0.15625
Outputs:
- factor: bfloat16 [16384, 2048], P('row', 'col')
Inputs may be any that keep to these rules, and one draw needn't show every extreme that they name: `fill_mask`: each column panel's density of filled blocks is drawn for that column from 1/8 to 8/8. `col_rows`: exactly 1 entries lie in each aligned run of 8 slabs.
All inputs are finite; a program needn't handle non-finite values.
Results may differ from a plain program's by a relative error of at most 0.0035.
Values may be sent and summed in bfloat16 or wider, within the bound.
No kernel may reach another device: no remote copies, remote signals or barrier semaphores. Data moves between devices by JAX's collectives and lax.ppermute only.
A program may use at most 64 MiB of HBM per device.

v0:
```python
import jax
import jax.numpy as jnp
from jax import lax
from jax.sharding import PartitionSpec as P

RB = 256
PW = 128


def from_root(shard, axis, root):
    mine = lax.axis_index(axis) == root
    return lax.psum(jnp.where(mine, shard, jnp.zeros_like(shard)), axis)


def contract(left, right):
    return lax.dot_general(
        left, right, (((1,), (1,)), ((), ())), preferred_element_type=jnp.float32
    )


def fetch_slabs(panel_tiles, col_rows):
    row_count = lax.axis_size("row")
    row_index = lax.axis_index("row")
    col_index = lax.axis_index("col")
    slab_tiles = panel_tiles.reshape(-1, PW, PW)
    per_device = slab_tiles.shape[0]
    all_cols = col_rows.shape[0]
    col_panels = all_cols // lax.axis_size("col")
    owner_row = col_rows // per_device
    slab_place = col_rows % per_device
    per_owner = all_cols // row_count
    position = jnp.arange(all_cols, dtype=jnp.int32)
    earlier = (owner_row[None, :] == owner_row[:, None]) & (position[None, :] < position[:, None])
    slab_rank = jnp.sum(earlier.astype(jnp.int32), axis=1)
    is_owned = (owner_row == row_index).astype(jnp.int32)
    rank_match = (slab_rank[:, None] == jnp.arange(per_owner, dtype=jnp.int32)[None, :]).astype(
        jnp.int32
    ) * is_owned[:, None]
    place_match = (slab_place[:, None] == jnp.arange(per_device, dtype=jnp.int32)[None, :]).astype(
        jnp.int32
    )
    select_table = jnp.dot(rank_match.T, place_match).astype(jnp.bfloat16)
    owned_slabs = jnp.einsum(
        "qs,sij->qij", select_table, slab_tiles, preferred_element_type=jnp.float32
    ).astype(jnp.bfloat16)
    everyone = lax.all_gather(owned_slabs, "row", axis=0, tiled=True)
    wanted_owner = lax.dynamic_slice_in_dim(owner_row, col_index * col_panels, col_panels)
    wanted_rank = lax.dynamic_slice_in_dim(slab_rank, col_index * col_panels, col_panels)
    gather_slot = wanted_owner * per_owner + wanted_rank
    pick_table = (
        gather_slot[:, None] == jnp.arange(row_count * per_owner, dtype=jnp.int32)[None, :]
    ).astype(jnp.bfloat16)
    result = jnp.einsum(
        "tq,qij->tij", pick_table, everyone, preferred_element_type=jnp.float32
    ).astype(jnp.bfloat16)
    return result


def shards(matrix, fill_mask, col_rows, inverses):
    col_index = lax.axis_index("col")
    local_rows = matrix.shape[0]
    width = matrix.shape[1]
    col_panels = fill_mask.shape[1]
    rows_mask = jnp.repeat(fill_mask.astype(jnp.float32), RB, axis=0)
    first_local = (
        jnp.dot(matrix[:, :PW], jnp.triu(inverses[0]), preferred_element_type=jnp.float32)
        * rows_mask[:, 0:1]
    ).astype(jnp.bfloat16)
    first_panel = from_root(first_local, "col", 0)
    diag_first = fetch_slabs(first_panel, col_rows)
    column_sum = matrix[:, :PW].astype(jnp.float32) - contract(first_panel, diag_first[0])
    panel_update = column_sum.astype(jnp.bfloat16)
    second_local = (
        jnp.dot(panel_update, jnp.triu(inverses[1]), preferred_element_type=jnp.float32)
        * rows_mask[:, 0:1]
    ).astype(jnp.bfloat16)
    second_panel = from_root(second_local, "col", 1)
    diag_second = fetch_slabs(second_panel, col_rows)
    both_panels = jnp.concatenate((first_panel, second_panel), axis=1)
    both_diag = jnp.concatenate((diag_first, diag_second), axis=2).reshape(-1, 2 * PW)
    schur_sum = matrix.astype(jnp.float32) - contract(both_panels, both_diag)
    masked = (
        (schur_sum.reshape(local_rows, col_panels, PW) * rows_mask[:, :, None])
        .astype(jnp.bfloat16)
        .reshape(local_rows, width)
    )
    leading = jnp.where(
        col_index == 0, first_panel, jnp.where(col_index == 1, second_panel, masked[:, :PW])
    )
    return jnp.concatenate((leading, masked[:, PW:]), axis=1)


def solution(mesh):
    in_specs = (P("row", "col"), P("row", "col"), P(), P())
    out_specs = P("row", "col")
    return jax.shard_map(shards, mesh=mesh, in_specs=in_specs, out_specs=out_specs, check_vma=False)
```

profile of v0, /device:TPU:0, one launch (start us, length us, event | category | flops | bytes accessed | tf_op | source)
XLA Modules:
  0.0 149.6 jit_solution(10960983689356108654)
XLA Ops:
  6.5 0.0 all-reduce.3.cloned.1.call-start
  6.5 0.7 convert_element_type.58
  7.3 0.1 broadcast_in_dim.8
  7.3 2.0 %fusion.6 = bf16[1024,128]{0,1:T(8,128)(2,1)} fusion(f32[1024]{0:T(1024)S(1)} %bitcast.68, pred[]{:T(512)S(6)} %eq.32, bf16[1024,1024]{1,0:T(8,128)(2,1)} %param.4, bf16[2,128,128]{2,1,0:T(8,128)(2,1)} %param.7, s32[128]{0:T(128)S(1)} %iota_add_fusion), kind=kOutput, calls=%fused_computation.13 | convolution fusion | flops 33980416 | bytes 561665 | tf_op jit(solution)/shard_map/dot_general | solution.py:66
  9.3 0.0 all-reduce.3.cloned.1.call-update
  9.4 0.0 all-reduce.5.cloned.1.call-start
  9.4 0.7 and_select_fusion.1
  10.1 0.2 convert_reduce_fusion
  10.3 0.1 dynamic-slice_add_fusion
  10.3 0.2 convolution_bitcast_fusion
  10.5 20.1 %all-reduce.3.cloned.1.call-done = bf16[1024,128]{0,1:T(8,128)(2,1)} async-done(((bf16[1024,128]{0,1:T(8,128)(2,1)}), bf16[1024,128]{0,1:T(8,128)(2,1)}) %all-reduce.3.cloned.1.call-update) | async-done | bytes 262160 | tf_op jit(solution)/shard_map/psum | solution.py:12
  30.7 1.1 copy.24
  31.8 0.2 fusion.47
  32.0 0.1 copy.20
  32.1 44.0 %all-gather = bf16[2048,128]{1,0:T(8,128)(2,1)S(1)} all-gather(bf16[128,128]{1,0:T(8,128)(2,1)S(1)} %bitcast.66), channel_id=2, replica_groups=mesh['row'=16,'col'=2] {'row'}, dimensions={0}, use_global_device_ids=true | all-gather | bytes 557056 | tf_op jit(solution)/shard_map/all_gather | solution.py:46
  76.1 0.4 convolution_convert_fusion.1
  76.6 2.1 %fusion.4 = bf16[1024,128]{0,1:T(8,128)(2,1)} fusion(bf16[1024,128]{0,1:T(8,128)(2,1)S(1)} %copy-done, f32[1024]{0:T(1024)S(1)} %bitcast.69, pred[]{:T(512)S(6)} %eq.33, bf16[1024,1024]{1,0:T(8,128)(2,1)} %param.4, bf16[1,128,128]{2,0,1:T(2,128)(2,1)S(1)} %slice.31, bf16[2,128,128]{2,1,0:T(8,128)(2,1)S(1)} %copy-done.2, s32[128]{0:T(128)S(1)} %iota_add_fusion), kind=kOutput, calls=%fused_computation.11 | convolution fusion | flops 67928064 | bytes 889345 | tf_op jit(solution)/shard_map/dot_general | solution.py:74
  78.7 0.0 all-reduce.5.cloned.1.call-update
  78.7 2.9 %copy.16 = bf16[1024,1024]{0,1:T(8,128)(2,1)S(1)} copy(bf16[1024,1024]{1,0:T(8,128)(2,1)} %param.4) | data formatting | bytes 4194304 | tf_op args[0]
  81.6 11.4 %all-reduce.5.cloned.1.call-done = bf16[1024,128]{0,1:T(8,128)(2,1)} async-done(((bf16[1024,128]{0,1:T(8,128)(2,1)}), bf16[1024,128]{0,1:T(8,128)(2,1)}) %all-reduce.5.cloned.1.call-update) | async-done | bytes 262160 | tf_op jit(solution)/shard_map/psum | solution.py:12
  93.0 1.1 copy.25
  94.1 0.2 fusion.48
  94.3 0.1 copy.22
  94.4 44.0 %all-gather.1 = bf16[2048,128]{1,0:T(8,128)(2,1)S(1)} all-gather(bf16[128,128]{1,0:T(8,128)(2,1)S(1)} %bitcast.67), channel_id=3, replica_groups=mesh['row'=16,'col'=2] {'row'}, dimensions={0}, use_global_device_ids=true | all-gather | bytes 557056 | tf_op jit(solution)/shard_map/all_gather | solution.py:46
  138.4 0.4 convolution_convert_fusion
  138.8 0.1 pad_maximum_fusion.1
  138.9 0.1 copy.18
  139.0 0.7 fusion
  139.8 0.1 slice.33
  139.9 0.1 fusion.13
  140.0 0.2 pad_maximum_fusion
  140.2 2.6 %copy.19 = bf16[1024,1024]{1,0:T(8,128)(2,1)} copy(bf16[1024,1024]{0,1:T(8,128)(2,1)S(1)} %pad_maximum_fusion) | data formatting | bytes 4194304 | tf_op jit(solution)/shard_map/concatenate | solution.py:90
  (9 shorter events, 0.1 us)
Async XLA Ops:
  6.5 70.0 %copy-start.2 = (bf16[2,128,128]{2,1,0:T(8,128)(2,1)S(1)}, bf16[2,128,128]{2,1,0:T(8,128)(2,1)}, u32[]{:S(2)}) copy-start(bf16[2,128,128]{2,1,0:T(8,128)(2,1)} %param.7) | copy-start | bytes 196612
  6.5 24.1 %all-reduce.3.cloned.1.call-start = ((), (), s32[]{:S(2)}) async-start(), calls=%async_computation | async-start | bytes 524288 | tf_op jit(solution)/shard_map/psum | solution.py:12
  9.4 83.7 %all-reduce.5.cloned.1.call-start = ((), (), s32[]{:S(2)}) async-start(), calls=%async_computation.1 | async-start | bytes 524288 | tf_op jit(solution)/shard_map/psum | solution.py:12
  30.7 45.9 %copy-start = (bf16[1024,128]{0,1:T(8,128)(2,1)S(1)}, bf16[1024,128]{0,1:T(8,128)(2,1)}, u32[]{:S(2)}) copy-start(bf16[1024,128]{0,1:T(8,128)(2,1)} %all-reduce.3.cloned.1.call-done) | copy-start | bytes 786436
  93.0 46.0 %copy-start.1 = (bf16[1024,128]{0,1:T(8,128)(2,1)S(1)}, bf16[1024,128]{0,1:T(8,128)(2,1)}, u32[]{:S(2)}) copy-start(bf16[1024,128]{0,1:T(8,128)(2,1)} %all-reduce.5.cloned.1.call-done) | copy-start | bytes 786436
Sparse Core Ops, SparseCore 0:
  9.7 20.9 all-reduce.2
  78.8 14.1 all-reduce.4
where the time goes:
time: 150 us
  blocking collectives  88 us (59%)
  waiting for transfers between devices  31.6 us (21%)
  between operations  13.5 us (9%)
  local copies, waits for them, and re-layouts  8.17 us (5%)
  matrix products  6.28 us (4%)
  other arithmetic  1.96 us (1%)
    all_gather x2, blocking collectives, fetch_slabs(): everyone = lax.all_gather(owned_slabs, 'row', axis=0, tiled=True)  88 us
    psum x2, waiting for transfers between devices, from_root(): return lax.psum(jnp.where(mine, shard, jnp.zeros_like(shard)), axis)  31.6 us
    unnamed x9, local copies, waits for them, and re-layouts  5.01 us
  transfers between devices with their start and end apart: 2, of which 2 were waited for; matrix products, arithmetic and copies ran while one was open for 3% of the time, Pallas kernels for 0%

commit v1 on v0

--- a/solution.py
+++ b/solution.py
@@ -9,7 +9,7 @@
 
 def from_root(shard, axis, root):
     mine = lax.axis_index(axis) == root
-    return lax.psum(jnp.where(mine, shard, jnp.zeros_like(shard)), axis)
+    return jnp.sum(lax.all_gather(jnp.where(mine, shard, jnp.zeros_like(shard)), axis), axis=0)
 
 
 def contract(left, right):

time: 150 us -> 102 us (0.68)
  waiting for transfers between devices: 31.6 us -> 0 us
  between operations: 13.5 us -> 0.16 us
  local copies, waits for them, and re-layouts: 8.17 us -> 2.89 us
  other arithmetic: 1.96 us -> 5 us
    psum x2 -> x0, waiting for transfers between devices: 31.6 us -> none  [from_root(): return lax.psum(jnp.where(mine, shard, jnp.zeros_like(shard)), axis)]
    unnamed x9 -> x5, local copies, waits for them, and re-layouts: 5.01 us -> 0.51 us
    all_gather x0 -> x2, blocking collectives: none -> 4.44 us  [from_root(): lax.all_gather(jnp.where(mine, shard, jnp.zeros_like(shard)), axis)]
    all_gather x2, blocking collectives: 88 us -> 83.7 us  [fetch_slabs(): everyone = lax.all_gather(owned_slabs, 'row', axis=0, tiled=True)]
    concatenate x1 -> x0, local copies, waits for them, and re-layouts: 2.56 us -> none  [shards(): return jnp.concatenate((leading, masked[:, PW:]), axis=1)]
    reduce_sum x0 -> x2, other arithmetic: none -> 1.58 us  [from_root(): jnp.sum(lax.all_gather(jnp.where(mine, shard, jnp.zeros_like(shard)), axi...]
  transfers between devices with their start and end apart: 2 -> 0, of which waited for: 2 -> 0; matrix products, arithmetic and copies ran while one was open for 3% -> 0% of each run, Pallas kernels for 0% -> 0%
where the time goes in v1:
time: 102 us
  blocking collectives  88.2 us (86%)
  matrix products  5.29 us (5%)
  other arithmetic  5 us (5%)
  local copies, waits for them, and re-layouts  2.89 us (3%)
    all_gather x2, blocking collectives, fetch_slabs(): everyone = lax.all_gather(owned_slabs, 'row', axis=0, tiled=True)  83.7 us
    all_gather x2, blocking collectives, from_root(): lax.all_gather(jnp.where(mine, shard, jnp.zeros_like(shard)), axis)  4.44 us

profile of v1, /device:TPU:0, one launch (start us, length us, event | category | flops | bytes accessed | tf_op | source)
XLA Modules:
  0.0 101.5 jit_solution(10553827772700376486)
XLA Ops:
  0.0 0.7 and_select_fusion.1
  0.7 0.2 convert_reduce_fusion
  0.9 0.2 convolution_bitcast_fusion
  1.1 0.1 dynamic-slice_add_fusion
  1.1 0.7 convert_element_type.62
  1.8 0.1 broadcast_in_dim.8
  1.9 1.3 %fusion.6 = bf16[1024,128]{0,1:T(8,128)(2,1)S(1)} fusion(f32[1024]{0:T(1024)S(1)} %bitcast.68, pred[]{:T(512)S(6)} %eq.32, bf16[1024,1024]{1,0:T(8,128)(2,1)} %param.4, bf16[2,128,128]{2,1,0:T(8,128)(2,1)} %param.7, s32[128]{0:T(128)S(1)} %iota_add_fusion), kind=kOutput, calls=%fused_computation.13 | convolution fusion | flops 33980416 | bytes 561665 | tf_op jit(solution)/shard_map/dot_general | solution.py:66
  3.2 2.3 %all-gather = bf16[2048,128]{0,1:T(8,128)(2,1)S(1)} all-gather(bf16[1024,128]{0,1:T(8,128)(2,1)S(1)} %fusion.6), channel_id=2, replica_groups=mesh['row'=16,'col'=2] {'col'}, dimensions={0}, use_global_device_ids=true | all-gather | bytes 786432 | tf_op jit(solution)/shard_map/all_gather | solution.py:12
  5.5 0.4 reshape.39
  5.8 0.0 copy-start.1
  5.8 1.4 %reduce_sum.37 = bf16[1024,128]{0,1:T(8,128)(2,1)S(1)} reduce(bf16[2,1024,128]{1,0,2:T(2,128)(2,1)S(1)} %reshape.39, bf16[]{:T(256)} %constant.51.clone.1), dimensions={0}, to_apply=%region_0.1 | reduce | flops 131072 | bytes 786434 | tf_op jit(solution)/shard_map/reduce_sum | solution.py:12
  7.2 0.2 copy.24
  7.4 0.1 copy.30
  7.5 0.2 fusion.49
  7.7 0.1 copy.25
  7.8 45.5 %all-gather.1 = bf16[2048,128]{1,0:T(8,128)(2,1)S(1)} all-gather(bf16[128,128]{1,0:T(8,128)(2,1)S(1)} %bitcast.67), channel_id=3, replica_groups=mesh['row'=16,'col'=2] {'row'}, dimensions={0}, use_global_device_ids=true | all-gather | bytes 557056 | tf_op jit(solution)/shard_map/all_gather | solution.py:46
  53.3 0.4 convolution_convert_fusion.1
  53.7 1.4 %fusion.4 = bf16[1024,128]{1,0:T(8,128)(2,1)S(1)} fusion(bf16[1024,128]{0,1:T(8,128)(2,1)S(1)} %reduce_sum.37, f32[1024]{0:T(1024)S(1)} %bitcast.69, pred[]{:T(512)S(6)} %eq.33, bf16[1024,1024]{1,0:T(8,128)(2,1)} %param.4, bf16[1,128,128]{2,0,1:T(2,128)(2,1)S(1)} %slice.31, bf16[2,128,128]{2,1,0:T(8,128)(2,1)S(1)} %copy-done.1, s32[128]{0:T(128)S(1)} %iota_add_fusion), kind=kOutput, calls=%fused_computation.11 | convolution fusion | flops 67928064 | bytes 889345 | tf_op jit(solution)/shard_map/dot_general | solution.py:74
  55.1 2.2 %all-gather.2 = bf16[2048,128]{1,0:T(8,128)(2,1)S(1)} all-gather(bf16[1024,128]{1,0:T(8,128)(2,1)S(1)} %fusion.4), channel_id=4, replica_groups=mesh['row'=16,'col'=2] {'col'}, dimensions={0}, use_global_device_ids=true | all-gather | bytes 786432 | tf_op jit(solution)/shard_map/all_gather | solution.py:12
  57.3 0.2 reduce_sum.39
  57.5 0.3 fusion.14
  57.8 38.3 %all-gather.3 = bf16[2048,128]{1,0:T(8,128)(2,1)S(1)} all-gather(bf16[128,128]{1,0:T(8,128)(2,1)S(1)} %convert_element_type.73), channel_id=5, replica_groups=mesh['row'=16,'col'=2] {'row'}, dimensions={0}, use_global_device_ids=true | all-gather | bytes 557056 | tf_op jit(solution)/shard_map/all_gather | solution.py:46
  96.0 0.4 convolution_convert_fusion
  96.4 0.1 pad_maximum_fusion.1
  96.5 0.1 copy.21
  96.6 0.2 copy.23
  96.8 1.1 %mul.47 = f32[1024,8,128]{2,1,0:T(8,128)S(1)} broadcast(f32[1024,8]{1,0:T(8,128)S(1)} %copy.23), dimensions={0,1} | broadcast | bytes 4227072 | tf_op jit(solution)/shard_map/mul | solution.py:83
  98.0 0.4 copy-done
  98.4 1.2 %fusion = bf16[1024,1024]{1,0:T(8,128)(2,1)S(1)} fusion(f32[128,8,8,128]{3,2,1,0:T(8,128)S(1)} %bitcast.56, bf16[1024,1024]{1,0:T(8,128)(2,1)S(1)} %copy-done, bf16[1024,256]{1,0:T(8,128)(2,1)S(1)} %bitcast.59, bf16[1024,128]{1,0:T(8,128)(2,1)S(1)} %reduce_sum.39, bf16[1024,128]{1,0:T(8,128)(2,1)S(1)} %copy.24), kind=kOutput, calls=%fused_computation.1 | convolution fusion | flops 542113792 | bytes 9437184 | tf_op jit(solution)/shard_map/dot_general | solution.py:16
  99.6 0.1 fusion.13
  99.7 0.2 slice.33
  99.9 1.6 %pad_maximum_fusion = bf16[1024,1024]{1,0:T(8,128)(2,1)} fusion(bf16[1024,896]{1,0:T(8,128)(2,1)S(1)} %slice.33, bf16[1024,128]{1,0:T(8,128)(2,1)S(1)} %fusion.13), kind=kLoop, calls=%fused_computation.2 | loop fusion | flops 4194304 | bytes 4194304 | tf_op jit(solution)/shard_map/concatenate | solution.py:90
  (6 shorter events, 0.1 us)
Async XLA Ops:
  5.8 47.9 %copy-start.1 = (bf16[2,128,128]{2,1,0:T(8,128)(2,1)S(1)}, bf16[2,128,128]{2,1,0:T(8,128)(2,1)}, u32[]{:S(2)}) copy-start(bf16[2,128,128]{2,1,0:T(8,128)(2,1)} %param.7) | copy-start | bytes 196612
  96.8 1.6 %copy-start = (bf16[1024,1024]{1,0:T(8,128)(2,1)S(1)}, bf16[1024,1024]{1,0:T(8,128)(2,1)}, u32[]{:S(2)}) copy-start(bf16[1024,1024]{1,0:T(8,128)(2,1)} %param.4) | copy-start | bytes 6291460
